TPU v7x, 32 devices: a whole 2x2x4 slice. The times are simulated.
32 devices in a mesh: dp: 8 (over z, x), tensor: 4 (over y, core).
Axes of the slice: x: 2, y: 2, z: 4, core: 2. Of those that a mesh axis runs over, the one named last changes fastest.
Arguments:
- tokens: bfloat16 [2048, 4096], P('dp', 'tensor'), may hold values from -6 to 6
- norm_gain: float32 [4096], replicated, may hold values from 0.15 to 5.4, as said below
- w_query: bfloat16 [4096, 4096], P(None, 'tensor'), may hold values from -0.09375 to 0.09375
- key_weight: bfloat16 [4096, 1024], P(None, 'tensor'), may hold values from -0.09375 to 0.09375
- value_weight: bfloat16 [4096, 1024], P(None, 'tensor'), may hold values from -0.09375 to 0.09375
- w_out: bfloat16 [4096, 4096], P('tensor'), may hold values from -0.25 to 0.25
- grad_output: bfloat16 [2048, 4096], P('dp', 'tensor'), may hold values from -6 to 6
- doc_lengths: int32 [8, 2], P('dp'), may hold values from 0 to 256, as said below
- block_owner: int32 [8, 8], replicated, may hold values from 0 to 7, as said below
Outputs:
- relaid_output: bfloat16 [2048, 4096], P('dp', 'tensor')
- input_grad: bfloat16 [2048, 4096], P('dp', 'tensor')
Inputs may be any that keep to these rules, and one draw needn't show every extreme that they name: `doc_lengths`: each row lists the lengths of the documents packed on that dp index in order: multiples of 128, the nonzero ones first, summing to 256. In every draw some dp index holds a single document of 256 tokens. `block_owner`: every dp index owns exactly one block of each position j < 8 and exactly one block from each dp index. `norm_gain`: positive gains.
All inputs are finite; a program needn't handle non-finite values.
Results may differ from a plain program's by a relative error of at most 0.015.
Values may be sent and summed in bfloat16 or wider, within the bound.
No kernel may reach another device: no remote copies, remote signals or barrier semaphores. Data moves between devices by JAX's collectives and lax.ppermute only.
A program may use at most 128 MiB of HBM per device.

v0:
```python
import math
import jax
import jax.numpy as jnp
from jax import lax
from jax.sharding import PartitionSpec as P

HEAD_SIZE = 128
ROPE_BASE = 500000.0
NORM_EPSILON = 1e-05


def doc_tables(lengths_row, token_row_count):
    ends = jnp.cumsum(lengths_row)
    token_index = jnp.arange(token_row_count, dtype=jnp.int32)
    passed = (token_index[:, None] >= ends[None, :]).astype(jnp.int32)
    doc_ids = jnp.sum(passed, axis=1)
    starts = jnp.max(jnp.where(passed > 0, ends[None, :], 0), axis=1)
    return (doc_ids, token_index - starts)


def rope_tables(positions, head_size):
    half_dim = head_size // 2
    steps = jnp.arange(half_dim, dtype=jnp.float32)
    inverse_freq = jnp.power(ROPE_BASE, -2.0 * steps / head_size)
    angles = positions.astype(jnp.float32)[:, None] * inverse_freq[None, :]
    return (jnp.cos(angles), jnp.sin(angles))


def rotate(vectors, cosine, sine_table):
    half_dim = vectors.shape[-1] // 2
    former = vectors[..., :half_dim]
    latter = vectors[..., half_dim:]
    cos_part = cosine[:, None, :]
    sin_part = sine_table[:, None, :]
    return jnp.concatenate(
        [former * cos_part - latter * sin_part, latter * cos_part + former * sin_part], axis=-1
    )


def unrotate(vectors, cosine, sine_table):
    half_dim = vectors.shape[-1] // 2
    former = vectors[..., :half_dim]
    latter = vectors[..., half_dim:]
    cos_part = cosine[:, None, :]
    sin_part = sine_table[:, None, :]
    return jnp.concatenate(
        [former * cos_part + latter * sin_part, latter * cos_part - former * sin_part], axis=-1
    )


def per_device(
    tokens,
    norm_gain,
    w_query,
    key_weight,
    value_weight,
    w_out,
    grad_output,
    doc_lengths,
    block_owner,
):
    token_row_count, width_part = tokens.shape
    full_width = norm_gain.shape[0]
    sources = lax.axis_size("dp")
    data_index = lax.axis_index("dp")
    tensor_index = lax.axis_index("tensor")
    query_width = w_query.shape[1]
    key_width = key_weight.shape[1]
    heads_local = query_width // HEAD_SIZE
    kv_local = key_width // HEAD_SIZE
    query_group_width = heads_local // kv_local
    scale_factor = 1.0 / math.sqrt(HEAD_SIZE)
    gain_part = lax.dynamic_slice_in_dim(norm_gain, tensor_index * width_part, width_part)
    w_joined = jnp.concatenate([w_query, key_weight, value_weight], axis=1)
    x_float = tokens.astype(jnp.float32)
    gathered = lax.all_gather(tokens, "tensor", axis=1, tiled=True)
    gathered_float = gathered.astype(jnp.float32)
    inverse = lax.rsqrt(jnp.mean(gathered_float * gathered_float, axis=1) + NORM_EPSILON)
    normed_input = (gathered_float * inverse[:, None] * norm_gain[None, :]).astype(jnp.bfloat16)
    projected = jnp.dot(normed_input, w_joined, preferred_element_type=jnp.float32)
    doc_ids, positions = doc_tables(doc_lengths[0], token_row_count)
    token_index = jnp.arange(token_row_count, dtype=jnp.int32)
    allowed = (doc_ids[:, None] == doc_ids[None, :]) & (
        token_index[None, :] <= token_index[:, None]
    )
    cosine, sine_table = rope_tables(positions, HEAD_SIZE)
    query_rows = rotate(
        projected[:, :query_width].reshape(token_row_count, heads_local, HEAD_SIZE),
        cosine,
        sine_table,
    ).astype(jnp.bfloat16)
    keys = rotate(
        projected[:, query_width : query_width + key_width].reshape(
            token_row_count, kv_local, HEAD_SIZE
        ),
        cosine,
        sine_table,
    ).astype(jnp.bfloat16)
    value_rows = (
        projected[:, query_width + key_width :]
        .astype(jnp.bfloat16)
        .reshape(token_row_count, kv_local, HEAD_SIZE)
    )
    grouped_query = query_rows.reshape(token_row_count, kv_local, query_group_width, HEAD_SIZE)
    scores = (
        jnp.einsum("qkgd,skd->kgqs", grouped_query, keys, preferred_element_type=jnp.float32)
        * scale_factor
    )
    weights = jnp.where(allowed[None, None], jnp.exp(scores), 0.0)
    probs = weights / jnp.sum(weights, axis=-1, keepdims=True)
    probs_low = probs.astype(jnp.bfloat16)
    attended = jnp.einsum(
        "kgqs,skd->qkgd", probs_low, value_rows, preferred_element_type=jnp.float32
    ).astype(jnp.bfloat16)
    attended_flat = attended.reshape(token_row_count, query_width)
    mixed_turned = lax.psum_scatter(
        lax.dot_general(
            w_out, attended_flat, (((0,), (1,)), ((), ())), preferred_element_type=jnp.float32
        ).astype(jnp.bfloat16),
        "tensor",
        scatter_dimension=0,
        tiled=True,
    ).astype(jnp.float32)
    output_home = (x_float + mixed_turned.T).astype(jnp.bfloat16)
    block_count = block_owner.shape[1]
    owner_row = lax.dynamic_slice_in_dim(block_owner, data_index, 1, 0)[0]
    slot_index = jnp.arange(sources, dtype=jnp.int32)
    send_table = (owner_row[None, :] == slot_index[:, None]).astype(jnp.bfloat16)
    owned_flags = jnp.sum((block_owner == data_index).astype(jnp.int32), axis=1)
    owned_rank = jnp.cumsum(owned_flags) - owned_flags
    block_index = jnp.arange(block_count, dtype=jnp.int32)
    keep_table = (
        (owned_rank[None, :] == block_index[:, None]) & (owned_flags[None, :] > 0)
    ).astype(jnp.bfloat16)
    home_blocks = output_home.reshape(block_count, -1)
    outgoing = jnp.dot(send_table, home_blocks, preferred_element_type=jnp.float32).astype(
        jnp.bfloat16
    )
    incoming = lax.all_to_all(outgoing, "dp", split_axis=0, concat_axis=0, tiled=True)
    relaid = (
        jnp.dot(keep_table, incoming, preferred_element_type=jnp.float32)
        .astype(jnp.bfloat16)
        .reshape(token_row_count, width_part)
    )
    owned_blocks = grad_output.reshape(block_count, -1)
    returning = lax.dot_general(
        keep_table, owned_blocks, (((0,), (0,)), ((), ())), preferred_element_type=jnp.float32
    ).astype(jnp.bfloat16)
    arrived = lax.all_to_all(returning, "dp", split_axis=0, concat_axis=0, tiled=True)
    grad_home = (
        lax.dot_general(
            send_table, arrived, (((0,), (0,)), ((), ())), preferred_element_type=jnp.float32
        )
        .astype(jnp.bfloat16)
        .reshape(token_row_count, width_part)
    )
    attended_gradient = lax.dot_general(
        lax.all_gather(grad_home, "tensor", axis=1, tiled=True),
        w_out,
        (((1,), (1,)), ((), ())),
        preferred_element_type=jnp.float32,
    ).astype(jnp.bfloat16)
    grouped_gradient = attended_gradient.reshape(
        token_row_count, kv_local, query_group_width, HEAD_SIZE
    )
    delta = jnp.sum(grouped_gradient.astype(jnp.float32) * attended.astype(jnp.float32), axis=-1)
    grad_probs = jnp.einsum(
        "qkgd,skd->kgqs", grouped_gradient, value_rows, preferred_element_type=jnp.float32
    )
    grad_scores = (probs * (grad_probs - jnp.transpose(delta, (1, 2, 0))[..., None])).astype(
        jnp.bfloat16
    )
    grad_query_rot = (
        jnp.einsum("kgqs,skd->qkgd", grad_scores, keys, preferred_element_type=jnp.float32)
        * scale_factor
    )
    grad_keys_rot = (
        jnp.einsum("kgqs,qkgd->skd", grad_scores, grouped_query, preferred_element_type=jnp.float32)
        * scale_factor
    )
    value_gradient = jnp.einsum(
        "kgqs,qkgd->skd", probs_low, grouped_gradient, preferred_element_type=jnp.float32
    )
    grad_query = unrotate(
        grad_query_rot.reshape(token_row_count, heads_local, HEAD_SIZE), cosine, sine_table
    ).astype(jnp.bfloat16)
    key_gradient = unrotate(grad_keys_rot, cosine, sine_table).astype(jnp.bfloat16)
    joined_grad = jnp.concatenate(
        [
            grad_query.reshape(token_row_count, query_width),
            key_gradient.reshape(token_row_count, key_width),
            value_gradient.astype(jnp.bfloat16).reshape(token_row_count, key_width),
        ],
        axis=1,
    )
    normed_gradient = (
        lax.psum_scatter(
            lax.dot_general(
                w_joined, joined_grad, (((1,), (1,)), ((), ())), preferred_element_type=jnp.float32
            ).astype(jnp.bfloat16),
            "tensor",
            scatter_dimension=0,
            tiled=True,
        )
        .astype(jnp.float32)
        .T
    )
    stat = (
        lax.psum(jnp.sum(normed_gradient * gain_part[None, :] * x_float, axis=1), "tensor")
        / full_width
    )
    cubed = inverse * inverse * inverse
    grad_x = (
        grad_home.astype(jnp.float32)
        + inverse[:, None] * gain_part[None, :] * normed_gradient
        - x_float * cubed[:, None] * stat[:, None]
    )
    return (relaid, grad_x.astype(jnp.bfloat16))


def solution(mesh):
    placed = (
        P("dp", "tensor"),
        P(),
        P(None, "tensor"),
        P(None, "tensor"),
        P(None, "tensor"),
        P("tensor", None),
        P("dp", "tensor"),
        P("dp", None),
        P(),
    )
    return jax.shard_map(
        per_device,
        mesh=mesh,
        in_specs=placed,
        out_specs=(P("dp", "tensor"), P("dp", "tensor")),
        check_vma=False,
    )
```

profile of v0, /device:TPU:0, one launch (start us, length us, event | category | flops | bytes accessed | tf_op | source)
XLA Modules:
  0.0 188.4 jit_solution(454758210394766941)
XLA Ops:
  7.2 0.7 all-gather.3.cloned.1.call-update
  7.9 1.3 reshape.232
  9.2 0.8 convert_reduce_fusion
  10.0 0.2 reduce-window.16
  10.2 0.4 fusion.1
  10.6 0.6 broadcast.110
  11.1 1.1 reduce
  12.2 1.2 reshape.245
  13.4 7.3 %all-to-all-start.1 = ((bf16[8,2,16384]{2,1,0:T(2,128)(2,1)}), bf16[8,2,16384]{2,1,0:T(2,128)(2,1)S(1)}, u32[]{:S(2)}, u32[]{:S(2)}) async-start(bf16[8,2,16384]{2,1,0:T(2,128)(2,1)} %reshape.245), calls=%async_computation.2 | async-start | bytes 1048576 | tf_op jit(solution)/shard_map/all_to_all | solution.py:149
  20.7 0.2 reduce-window.17
  20.9 0.7 dynamic-slice_bitcast_fusion
  21.7 0.1 fusion.34
  21.8 7.9 %constant_dynamic-update-slice_fusion.2 = bf16[4096,1536]{1,0:T(8,128)(2,1)} fusion(bf16[4096,1024]{1,0:T(8,128)(2,1)} %param.11), kind=kLoop, calls=%fused_computation.78 | loop fusion | bytes 16777216
  29.7 1.6 constant_dynamic-update-slice_fusion.1
  31.3 0.8 copy-done.3
  32.1 1.7 constant_dynamic-update-slice_fusion
  33.8 1.4 all-to-all-done.1
  35.1 0.5 reshape.246
  35.7 0.7 convolution_convert_fusion
  36.4 1.0 reshape.233
  37.4 0.2 reduce-scatter.5.cloned.1.call-start
  37.7 0.5 multiply_cosine_fusion
  38.2 2.2 %fusion.3 = f32[256]{0:T(256)S(1)} fusion(bf16[256,4096]{1,0:T(8,128)(2,1)} %all-gather.3.cloned.1.call-done), kind=kLoop, calls=%fused_computation.11 | loop fusion | flops 3145472 | bytes 2098176 | tf_op jit(solution)/shard_map/reduce_sum | solution.py:78
  40.5 6.8 %fusion.6 = f32[256,1536]{1,0:T(8,128)S(1)} fusion(bf16[4096,1536]{1,0:T(8,128)(2,1)} %constant_dynamic-update-slice_fusion, bf16[256,4096]{1,0:T(8,128)(2,1)S(1)} %copy-done.4, f32[4096]{0:T(1024)S(1)} %copy-done.11, f32[256]{0:T(256)S(1)} %get-tuple-element.21), kind=kOutput, calls=%fused_computation.14 | convolution fusion | flops 3225419776 | bytes 16270336 | tf_op jit(solution)/shard_map/dot_general | solution.py:80
  47.5 0.2 copy.146
  47.7 0.9 copy-done.5
  48.6 0.5 subtract_convert_fusion.1
  49.2 0.3 slice-done
  49.5 0.1 reshape.227
  49.7 0.3 fusion.56
  50.1 2.1 %fusion.13 = (f32[2,4,256]{2,1,0:T(4,128)S(1)}, f32[2,256,256,4]{2,1,3,0:T(8,128)}) fusion(pred[256,256]{0,1:T(8,128)(4,1)S(1)} %fusion.34, bf16[256,2,4,64]{3,0,2,1:T(8,128)(2,1)S(1)} %bitcast.116, bf16[256,2,4,64]{3,0,2,1:T(8,128)(2,1)S(1)} %bitcast.118, bf16[256,2,64]{2,0,1:T(8,128)(2,1)S(1)} %get-tuple-element.11, ...), kind=kOutput, calls=%fused_computation.22 | convolution fusion | flops 137099264 | bytes 2826240 | tf_op jit(solution)/shard_map/qkgd,skd->kgqs/dot_general | solution.py:106
  52.2 8.0 %all-gather.5.cloned.1.call-done = bf16[256,4096]{1,0:T(8,128)(2,1)} async-done(((bf16[256,1024]{1,0:T(8,128)(2,1)}), bf16[256,4096]{1,0:T(8,128)(2,1)}) %all-gather.5.cloned.1.call-update) | async-done | bytes 2097168 | tf_op jit(solution)/shard_map/all_gather | solution.py:158
  60.2 6.4 %convolution_convert_fusion.6 = bf16[256,1024]{1,0:T(8,128)(2,1)S(1)} fusion(bf16[256,4096]{1,0:T(8,128)(2,1)} %all-gather.5.cloned.1.call-done, bf16[1024,4096]{1,0:T(8,128)(2,1)} %param.14), kind=kOutput, calls=%fused_computation.27 | convolution fusion | flops 2147745792 | bytes 11010048 | tf_op jit(solution)/shard_map/dot_general | solution.py:157
  66.6 0.2 copy.105
  66.8 2.4 %fusion.16 = bf16[2,128,256]{2,1,0:T(8,128)(2,1)S(1)} fusion(bf16[256,2,4,128]{0,3,2,1:T(8,128)(2,1)S(1)} %bitcast.121, f32[2,256,256,4]{2,1,3,0:T(8,128)} %get-tuple-element.23, f32[2,4,256]{2,1,0:T(4,128)S(1)} %get-tuple-element.22, pred[256,256]{0,1:T(8,128)(4,1)S(1)} %fusion.34), kind=kOutput, calls=%fused_computation.33 | convolution fusion | flops 136380416 | bytes 2826240 | tf_op jit(solution)/shard_map/kgqs,qkgd->skd/dot_general | solution.py:181
  69.3 1.6 multiply_reduce_fusion
  70.8 0.7 fusion.9
  71.6 0.5 fusion.15
  72.1 0.4 convolution_multiply_fusion
  72.6 0.2 add_convert_fusion.2
  72.8 0.1 pad_maximum_fusion.2
  72.9 0.1 copy.115
  73.0 0.8 copy.117
  73.9 0.4 copy.145
  74.3 0.4 copy.144
  74.7 0.3 add_convert_fusion
  75.0 0.3 pad_maximum_fusion.1
  75.4 0.5 copy-done.6
  75.9 13.8 %convolution_convert_fusion.4 = bf16[4096,256]{0,1:T(8,128)(2,1)} fusion(bf16[4096,1536]{1,0:T(8,128)(2,1)} %constant_dynamic-update-slice_fusion, bf16[256,256]{1,0:T(8,128)(2,1)S(1)} %copy.118, bf16[256,256]{1,0:T(8,128)(2,1)S(1)} %copy-done.6, bf16[256,1024]{1,0:T(8,128)(2,1)S(1)} %bitcast.123), kind=kOutput, calls=%fused_computation.8 | convolution fusion | flops 3224633344 | bytes 15466496 | tf_op jit(solution)/shard_map/dot_general | solution.py:198
  89.8 7.1 %fusion.2 = bf16[4096,256]{0,1:T(8,128)(2,1)} fusion(bf16[256,1024]{0,1:T(8,128)(2,1)S(1)} %bitcast.120, bf16[1024,4096]{1,0:T(8,128)(2,1)} %param.14), kind=kOutput, calls=%fused_computation.10 | convolution fusion | flops 2148532224 | bytes 11010048 | tf_op jit(solution)/shard_map/dot_general | solution.py:117
  96.9 0.8 dynamic_slice.7
  97.7 23.6 %reduce-scatter.5.cloned.1.call-done = bf16[1024,256]{0,1:T(8,128)(2,1)} async-done(((bf16[4096,256]{0,1:T(8,128)(2,1)}), bf16[1024,256]{0,1:T(8,128)(2,1)}) %reduce-scatter.5.cloned.1.call-update) | async-done | bytes 524304 | tf_op jit(solution)/shard_map/reduce_scatter | solution.py:197
  121.3 1.3 fusion.21
  122.6 5.8 %psum.7 = f32[256]{0:T(256)S(1)} all-reduce(f32[256]{0:T(256)S(1)} %fusion.21), channel_id=1, replica_groups=mesh['dp'=8,'tensor'=4] {'tensor'}, use_global_device_ids=true, to_apply=%region_11.12 | all-reduce | flops 256 | bytes 2048 | tf_op jit(solution)/shard_map/psum | solution.py:209
  128.4 26.9 %reduce-scatter.3.cloned.1.call-done = bf16[1024,256]{0,1:T(8,128)(2,1)} async-done(((bf16[4096,256]{0,1:T(8,128)(2,1)}), bf16[1024,256]{0,1:T(8,128)(2,1)}) %reduce-scatter.3.cloned.1.call-update) | async-done | bytes 524304 | tf_op jit(solution)/shard_map/reduce_scatter | solution.py:116
  155.3 2.5 %fusion.20 = (bf16[256,1024]{1,0:T(8,128)(2,1)}, bf16[256,1024]{1,0:T(8,128)(2,1)S(1)}) fusion(bf16[256,1024]{1,0:T(8,128)(2,1)S(1)} %copy-done, bf16[1024,256]{0,1:T(8,128)(2,1)} %reduce-scatter.5.cloned.1.call-done, bf16[256,1024]{1,0:T(8,128)(2,1)S(1)} %copy-done.1, f32[256]{0:T(256)S(1)} %broadcast_multiply_fusion, f32[256]{0:T(256)S(1)} %get-tuple-element.20, ...), kind=kLoop, calls=%fused_computation.37 | loop fusion | flops 3407872 | bytes 3152896 | tf_op jit(solution)/shard_map/convert_element_type | solution.py:218
  157.8 0.2 reshape.230
  158.0 0.3 fusion
  158.3 1.1 reduce.1
  159.4 0.4 reshape.243
  159.8 19.9 %all_to_all.24 = bf16[8,2,16384]{2,1,0:T(2,128)(2,1)S(1)} all-to-all(bf16[8,2,16384]{2,1,0:T(2,128)(2,1)S(1)} %reshape.243), channel_id=1, replica_groups=mesh['dp'=8,'tensor'=4] {'dp'}, dimensions={0} | all-to-all | bytes 1048576 | tf_op jit(solution)/shard_map/all_to_all | solution.py:139
  179.6 0.5 reshape.244
  180.2 0.7 convolution_convert_fusion.2
  180.8 1.0 reshape.231
  (49 shorter events, 1.0 us)
Async XLA Ops:
  7.2 31.1 %all-gather.3.cloned.1.call-start = ((), (), s32[]{:S(2)}) async-start(), calls=%async_computation.4 | async-start | bytes 2621440 | tf_op jit(solution)/shard_map/all_gather | solution.py:76
  10.2 10.5 %copy-start.12 = (s32[1,2]{1,0:T(1,128)S(1)}, s32[1,2]{1,0:T(1,128)}, u32[]{:S(2)}) copy-start(s32[1,2]{1,0:T(1,128)} %param.16) | copy-start | bytes 28
  13.4 21.7 %all-to-all-start.1 = ((bf16[8,2,16384]{2,1,0:T(2,128)(2,1)}), bf16[8,2,16384]{2,1,0:T(2,128)(2,1)S(1)}, u32[]{:S(2)}, u32[]{:S(2)}) async-start(bf16[8,2,16384]{2,1,0:T(2,128)(2,1)} %reshape.245), calls=%async_computation.2 | async-start | bytes 1048576 | tf_op jit(solution)/shard_map/all_to_all | solution.py:149
  20.6 39.6 %all-gather.5.cloned.1.call-start = ((), (), s32[]{:S(2)}) async-start(), calls=%async_computation.6 | async-start | bytes 2621440 | tf_op jit(solution)/shard_map/all_gather | solution.py:158
  21.6 14.1 %copy-start.9 = (s32[8]{0:T(128)}, s32[8]{0:T(128)S(1)}, u32[]{:S(2)}) copy-start(s32[8]{0:T(128)S(1)} %dynamic-slice_bitcast_fusion) | copy-start | bytes 100
  21.8 45.1 %copy-start.7 = (pred[256,256]{0,1:T(8,128)(4,1)}, pred[256,256]{0,1:T(8,128)(4,1)S(1)}, u32[]{:S(2)}) copy-start(pred[256,256]{0,1:T(8,128)(4,1)S(1)} %fusion.34) | copy-start | bytes 196612
  21.8 7.9 %copy-start.2 = (bf16[4096,256]{1,0:T(8,128)(2,1)S(1)}, bf16[4096,256]{1,0:T(8,128)(2,1)}, u32[]{:S(2)}) copy-start(bf16[4096,256]{1,0:T(8,128)(2,1)} %param.12) | copy-start | bytes 6291460
  29.7 2.4 %copy-start.3 = (bf16[4096,256]{1,0:T(8,128)(2,1)S(1)}, bf16[4096,256]{1,0:T(8,128)(2,1)}, u32[]{:S(2)}) copy-start(bf16[4096,256]{1,0:T(8,128)(2,1)} %param.13) | copy-start | bytes 6291460
  36.4 4.1 %copy-start.11 = (f32[4096]{0:T(1024)S(1)}, f32[4096]{0:T(1024)}, u32[]{:S(2)}) copy-start(f32[4096]{0:T(1024)} %param.10) | copy-start | bytes 49156
  37.4 83.9 %reduce-scatter.5.cloned.1.call-start = ((), (), s32[]{:S(2)}) async-start(), calls=%async_computation.7 | async-start | bytes 2621440 | tf_op jit(solution)/shard_map/reduce_scatter | solution.py:197
  38.2 2.3 %copy-start.4 = (bf16[256,4096]{1,0:T(8,128)(2,1)S(1)}, bf16[256,4096]{1,0:T(8,128)(2,1)}, u32[]{:S(2)}) copy-start(bf16[256,4096]{1,0:T(8,128)(2,1)} %all-gather.3.cloned.1.call-done) | copy-start | bytes 6291460
  47.4 1.2 copy-start.5
  48.6 0.9 slice-start
  66.8 2.4 %copy-start.13 = (f32[2,256,256,4]{2,1,3,0:T(8,128)S(1)}, f32[2,256,256,4]{2,1,3,0:T(8,128)}, u32[]{:S(2)}) copy-start(f32[2,256,256,4]{2,1,3,0:T(8,128)} %get-tuple-element.23) | copy-start | bytes 6291460
  69.2 1.6 copy-start.8
  75.0 0.9 copy-start.6
  89.7 65.6 %reduce-scatter.3.cloned.1.call-start = ((), (), s32[]{:S(2)}) async-start(), calls=%async_computation.5 | async-start | bytes 2621440 | tf_op jit(solution)/shard_map/reduce_scatter | solution.py:116
  96.9 24.4 %copy-start = (bf16[256,1024]{1,0:T(8,128)(2,1)S(1)}, bf16[256,1024]{1,0:T(8,128)(2,1)}, u32[]{:S(2)}) copy-start(bf16[256,1024]{1,0:T(8,128)(2,1)} %param.9) | copy-start | bytes 1572868
  96.9 58.4 %copy-start.1 = (bf16[256,1024]{1,0:T(8,128)(2,1)S(1)}, bf16[256,1024]{1,0:T(8,128)(2,1)}, u32[]{:S(2)}) copy-start(bf16[256,1024]{1,0:T(8,128)(2,1)} %reshape.233) | copy-start | bytes 1572868
  155.3 2.7 %copy-start.10 = (s32[8]{0:T(128)S(1)}, s32[8]{0:T(128)}, u32[]{:S(2)}) copy-start(s32[8]{0:T(128)} %copy-done.9) | copy-start | bytes 100
Sparse Core Ops, SparseCore 0:
  9.6 25.2 all-gather.2
  37.5 22.6 all-gather.4
  89.9 31.4 reduce-scatter.4
  123.9 31.3 reduce-scatter.2
where the time goes:
time: 189 us; the launch traced here: 188 us
  waiting for transfers between devices  60.6 us (32%)
  matrix products  43.8 us (23%)
  blocking collectives  25.6 us (14%)
  local copies, waits for them, and re-layouts  25.1 us (13%)
  between operations  14.2 us (8%)
  other arithmetic  11.4 us (6%)
  starting transfers between devices  7.59 us (4%)
    reduce_scatter x1, waiting for transfers between devices, per_device(): lax.psum_scatter(lax.dot_general(w_out, attended_flat, (((0,), (1,)), (()...  26.9 us
    reduce_scatter x1, waiting for transfers between devices, per_device(): lax.psum_scatter(lax.dot_general(w_joined, joined_grad, (((1,), (1,)), ((...  23.6 us
    all_to_all x1, blocking collectives, per_device(): lax.all_to_all(outgoing, 'dp', split_axis=0, concat_axis=0, tiled=True)  19.9 us
    unnamed x39, local copies, waits for them, and re-layouts  15.5 us
    dot_general x1, matrix products, per_device(): lax.dot_general(w_joined, joined_grad, (((1,), (1,)), ((), ())), preferre...  13.8 us
    all_gather x1, waiting for transfers between devices, per_device(): lax.all_gather(grad_home, 'tensor', axis=1, tiled=True)  7.99 us
    all_to_all x1, starting transfers between devices, per_device(): lax.all_to_all(returning, 'dp', split_axis=0, concat_axis=0, tiled=True)  7.25 us
    dot_general x1, matrix products, per_device(): lax.dot_general(w_out, attended_flat, (((0,), (1,)), ((), ())), preferred...  7.11 us
  transfers between devices with their start and end apart: 5, of which 4 were waited for; matrix products, arithmetic and copies ran while one was open for 23% of the time, Pallas kernels for 0%

commit v1 on v0

--- a/solution.py
+++ b/solution.py
@@ -206,7 +206,12 @@
         .T
     )
     stat = (
-        lax.psum(jnp.sum(normed_gradient * gain_part[None, :] * x_float, axis=1), "tensor")
+        jnp.sum(
+            lax.all_gather(
+                jnp.sum(normed_gradient * gain_part[None, :] * x_float, axis=1), "tensor"
+            ),
+            axis=0,
+        )
         / full_width
     )
     cubed = inverse * inverse * inverse

time: 189 us -> 189 us (level)
    psum x1 -> x0, blocking collectives: 5.76 us -> none  [per_device(): lax.psum(jnp.sum(normed_gradient * gain_part[None, :] * x_float, axis=1),...]
    all_gather x0 -> x1, blocking collectives: none -> 5.07 us  [per_device(): lax.all_gather(jnp.sum(normed_gradient * gain_part[None, :] * x_float, ax...]
where the time goes in v1:
time: 189 us; the launch traced here: 188 us
  waiting for transfers between devices  61.3 us (32%)
  matrix products  43.8 us (23%)
  local copies, waits for them, and re-layouts  25.1 us (13%)
  blocking collectives  24.9 us (13%)
  between operations  14.2 us (8%)
  other arithmetic  11.5 us (6%)
  starting transfers between devices  7.59 us (4%)
    reduce_scatter x1, waiting for transfers between devices, per_device(): lax.psum_scatter(lax.dot_general(w_out, attended_flat, (((0,), (1,)), (()...  27.6 us
    reduce_scatter x1, waiting for transfers between devices, per_device(): lax.psum_scatter(lax.dot_general(w_joined, joined_grad, (((1,), (1,)), ((...  23.6 us
    all_to_all x1, blocking collectives, per_device(): lax.all_to_all(outgoing, 'dp', split_axis=0, concat_axis=0, tiled=True)  19.9 us
    unnamed x39, local copies, waits for them, and re-layouts  15.5 us
    dot_general x1, matrix products, per_device(): lax.dot_general(w_joined, joined_grad, (((1,), (1,)), ((), ())), preferre...  13.8 us
    all_gather x1, waiting for transfers between devices, per_device(): lax.all_gather(grad_home, 'tensor', axis=1, tiled=True)  7.99 us
    all_to_all x1, starting transfers between devices, per_device(): lax.all_to_all(returning, 'dp', split_axis=0, concat_axis=0, tiled=True)  7.25 us
    dot_general x1, matrix products, per_device(): lax.dot_general(w_out, attended_flat, (((0,), (1,)), ((), ())), preferred...  7.11 us
  transfers between devices with their start and end apart: 5, of which 4 were waited for; matrix products, arithmetic and copies ran while one was open for 23% of the time, Pallas kernels for 0%

profile of v1, /device:TPU:0, one launch (start us, length us, event | category | flops | bytes accessed | tf_op | source)
XLA Modules:
  0.0 188.4 jit_solution(12962008922975050886)
XLA Ops:
  7.2 0.7 all-gather.5.cloned.1.call-update
  7.9 1.3 reshape.234
  9.2 0.8 convert_reduce_fusion
  10.0 0.2 reduce-window.16
  10.2 0.4 fusion.1
  10.6 0.6 broadcast.113
  11.1 1.1 reduce.1
  12.2 1.2 reshape.251
  13.4 7.3 %all-to-all-start.1 = ((bf16[8,2,16384]{2,1,0:T(2,128)(2,1)}), bf16[8,2,16384]{2,1,0:T(2,128)(2,1)S(1)}, u32[]{:S(2)}, u32[]{:S(2)}) async-start(bf16[8,2,16384]{2,1,0:T(2,128)(2,1)} %reshape.251), calls=%async_computation.2 | async-start | bytes 1048576 | tf_op jit(solution)/shard_map/all_to_all | solution.py:149
  20.7 0.2 reduce-window.17
  20.9 0.7 dynamic-slice_bitcast_fusion
  21.7 0.1 fusion.34
  21.8 7.9 %constant_dynamic-update-slice_fusion.2 = bf16[4096,1536]{1,0:T(8,128)(2,1)} fusion(bf16[4096,1024]{1,0:T(8,128)(2,1)} %param.11), kind=kLoop, calls=%fused_computation.78 | loop fusion | bytes 16777216
  29.7 1.6 constant_dynamic-update-slice_fusion.1
  31.3 0.8 copy-done.3
  32.1 1.7 constant_dynamic-update-slice_fusion
  33.8 1.4 all-to-all-done.1
  35.1 0.5 reshape.252
  35.7 0.7 convolution_convert_fusion
  36.4 1.0 reshape.235
  37.4 0.2 reduce-scatter.5.cloned.1.call-start
  37.7 0.5 multiply_cosine_fusion
  38.2 2.2 %fusion.3 = f32[256]{0:T(256)S(1)} fusion(bf16[256,4096]{1,0:T(8,128)(2,1)} %all-gather.5.cloned.1.call-done), kind=kLoop, calls=%fused_computation.11 | loop fusion | flops 3145472 | bytes 2098176 | tf_op jit(solution)/shard_map/reduce_sum | solution.py:78
  40.5 6.8 %fusion.6 = f32[256,1536]{1,0:T(8,128)S(1)} fusion(bf16[4096,1536]{1,0:T(8,128)(2,1)} %constant_dynamic-update-slice_fusion, bf16[256,4096]{1,0:T(8,128)(2,1)S(1)} %copy-done.4, f32[4096]{0:T(1024)S(1)} %copy-done.11, f32[256]{0:T(256)S(1)} %get-tuple-element.21), kind=kOutput, calls=%fused_computation.14 | convolution fusion | flops 3225419776 | bytes 16270336 | tf_op jit(solution)/shard_map/dot_general | solution.py:80
  47.5 0.2 copy.146
  47.7 0.9 copy-done.5
  48.6 0.5 subtract_convert_fusion.1
  49.2 0.3 slice-done
  49.5 0.1 reshape.229
  49.7 0.3 fusion.56
  50.1 2.1 %fusion.13 = (f32[2,4,256]{2,1,0:T(4,128)S(1)}, f32[2,256,256,4]{2,1,3,0:T(8,128)}) fusion(pred[256,256]{0,1:T(8,128)(4,1)S(1)} %fusion.34, bf16[256,2,4,64]{3,0,2,1:T(8,128)(2,1)S(1)} %bitcast.117, bf16[256,2,4,64]{3,0,2,1:T(8,128)(2,1)S(1)} %bitcast.119, bf16[256,2,64]{2,0,1:T(8,128)(2,1)S(1)} %get-tuple-element.11, ...), kind=kOutput, calls=%fused_computation.22 | convolution fusion | flops 137099264 | bytes 2826240 | tf_op jit(solution)/shard_map/qkgd,skd->kgqs/dot_general | solution.py:106
  52.2 8.0 %all-gather.7.cloned.1.call-done = bf16[256,4096]{1,0:T(8,128)(2,1)} async-done(((bf16[256,1024]{1,0:T(8,128)(2,1)}), bf16[256,4096]{1,0:T(8,128)(2,1)}) %all-gather.7.cloned.1.call-update) | async-done | bytes 2097168 | tf_op jit(solution)/shard_map/all_gather | solution.py:158
  60.2 6.4 %convolution_convert_fusion.6 = bf16[256,1024]{1,0:T(8,128)(2,1)S(1)} fusion(bf16[256,4096]{1,0:T(8,128)(2,1)} %all-gather.7.cloned.1.call-done, bf16[1024,4096]{1,0:T(8,128)(2,1)} %param.14), kind=kOutput, calls=%fused_computation.27 | convolution fusion | flops 2147745792 | bytes 11010048 | tf_op jit(solution)/shard_map/dot_general | solution.py:157
  66.6 0.2 copy.105
  66.8 2.4 %fusion.16 = bf16[2,128,256]{2,1,0:T(8,128)(2,1)S(1)} fusion(bf16[256,2,4,128]{0,3,2,1:T(8,128)(2,1)S(1)} %bitcast.122, f32[2,256,256,4]{2,1,3,0:T(8,128)} %get-tuple-element.23, f32[2,4,256]{2,1,0:T(4,128)S(1)} %get-tuple-element.22, pred[256,256]{0,1:T(8,128)(4,1)S(1)} %fusion.34), kind=kOutput, calls=%fused_computation.33 | convolution fusion | flops 136380416 | bytes 2826240 | tf_op jit(solution)/shard_map/kgqs,qkgd->skd/dot_general | solution.py:181
  69.3 1.6 multiply_reduce_fusion
  70.8 0.7 fusion.9
  71.6 0.5 fusion.15
  72.1 0.4 convolution_multiply_fusion
  72.6 0.2 add_convert_fusion.2
  72.8 0.1 pad_maximum_fusion.2
  72.9 0.1 copy.115
  73.0 0.8 copy.117
  73.9 0.4 copy.145
  74.3 0.4 copy.144
  74.7 0.3 add_convert_fusion
  75.0 0.3 pad_maximum_fusion.1
  75.4 0.5 copy-done.6
  75.9 13.8 %convolution_convert_fusion.4 = bf16[4096,256]{0,1:T(8,128)(2,1)} fusion(bf16[4096,1536]{1,0:T(8,128)(2,1)} %constant_dynamic-update-slice_fusion, bf16[256,256]{1,0:T(8,128)(2,1)S(1)} %copy.118, bf16[256,256]{1,0:T(8,128)(2,1)S(1)} %copy-done.6, bf16[256,1024]{1,0:T(8,128)(2,1)S(1)} %bitcast.124), kind=kOutput, calls=%fused_computation.8 | convolution fusion | flops 3224633344 | bytes 15466496 | tf_op jit(solution)/shard_map/dot_general | solution.py:198
  89.8 7.1 %fusion.2 = bf16[4096,256]{0,1:T(8,128)(2,1)} fusion(bf16[256,1024]{0,1:T(8,128)(2,1)S(1)} %bitcast.121, bf16[1024,4096]{1,0:T(8,128)(2,1)} %param.14), kind=kOutput, calls=%fused_computation.10 | convolution fusion | flops 2148532224 | bytes 11010048 | tf_op jit(solution)/shard_map/dot_general | solution.py:117
  96.9 0.8 dynamic_slice.7
  97.7 23.6 %reduce-scatter.5.cloned.1.call-done = bf16[1024,256]{0,1:T(8,128)(2,1)} async-done(((bf16[4096,256]{0,1:T(8,128)(2,1)}), bf16[1024,256]{0,1:T(8,128)(2,1)}) %reduce-scatter.5.cloned.1.call-update) | async-done | bytes 524304 | tf_op jit(solution)/shard_map/reduce_scatter | solution.py:197
  121.3 1.3 fusion.21
  122.6 5.1 %all-gather.1 = f32[4,1,256]{2,1,0:T(1,128)S(1)} all-gather(f32[1,1,256]{2,1,0:T(1,128)S(1)} %bitcast.129), channel_id=2, replica_groups=mesh['dp'=8,'tensor'=4] {'tensor'}, dimensions={0}, use_global_device_ids=true | all-gather | bytes 5120 | tf_op jit(solution)/shard_map/all_gather | solution.py:210
  127.7 27.6 %reduce-scatter.3.cloned.1.call-done = bf16[1024,256]{0,1:T(8,128)(2,1)} async-done(((bf16[4096,256]{0,1:T(8,128)(2,1)}), bf16[1024,256]{0,1:T(8,128)(2,1)}) %reduce-scatter.3.cloned.1.call-update) | async-done | bytes 524304 | tf_op jit(solution)/shard_map/reduce_scatter | solution.py:116
  155.3 2.5 %fusion.20 = (bf16[256,1024]{1,0:T(8,128)(2,1)}, bf16[256,1024]{1,0:T(8,128)(2,1)S(1)}) fusion(bf16[256,1024]{1,0:T(8,128)(2,1)S(1)} %copy-done, bf16[1024,256]{0,1:T(8,128)(2,1)} %reduce-scatter.5.cloned.1.call-done, bf16[256,1024]{1,0:T(8,128)(2,1)S(1)} %copy-done.1, f32[256]{0:T(256)S(1)} %broadcast_multiply_fusion, f32[256]{0:T(256)S(1)} %get-tuple-element.20, ...), kind=kLoop, calls=%fused_computation.37 | loop fusion | flops 3407872 | bytes 3152896 | tf_op jit(solution)/shard_map/convert_element_type | solution.py:223
  157.8 0.2 reshape.232
  158.0 0.3 fusion
  158.3 1.1 reduce.2
  159.4 0.4 reshape.249
  159.8 19.9 %all_to_all.24 = bf16[8,2,16384]{2,1,0:T(2,128)(2,1)S(1)} all-to-all(bf16[8,2,16384]{2,1,0:T(2,128)(2,1)S(1)} %reshape.249), channel_id=1, replica_groups=mesh['dp'=8,'tensor'=4] {'dp'}, dimensions={0} | all-to-all | bytes 1048576 | tf_op jit(solution)/shard_map/all_to_all | solution.py:139
  179.6 0.5 reshape.250
  180.2 0.7 convolution_convert_fusion.2
  180.8 1.0 reshape.233
  (50 shorter events, 1.0 us)
Async XLA Ops:
  7.2 31.1 %all-gather.5.cloned.1.call-start = ((), (), s32[]{:S(2)}) async-start(), calls=%async_computation.4 | async-start | bytes 2621440 | tf_op jit(solution)/shard_map/all_gather | solution.py:76
  10.2 10.5 %copy-start.12 = (s32[1,2]{1,0:T(1,128)S(1)}, s32[1,2]{1,0:T(1,128)}, u32[]{:S(2)}) copy-start(s32[1,2]{1,0:T(1,128)} %param.16) | copy-start | bytes 28
  13.4 21.7 %all-to-all-start.1 = ((bf16[8,2,16384]{2,1,0:T(2,128)(2,1)}), bf16[8,2,16384]{2,1,0:T(2,128)(2,1)S(1)}, u32[]{:S(2)}, u32[]{:S(2)}) async-start(bf16[8,2,16384]{2,1,0:T(2,128)(2,1)} %reshape.251), calls=%async_computation.2 | async-start | bytes 1048576 | tf_op jit(solution)/shard_map/all_to_all | solution.py:149
  20.6 39.6 %all-gather.7.cloned.1.call-start = ((), (), s32[]{:S(2)}) async-start(), calls=%async_computation.6 | async-start | bytes 2621440 | tf_op jit(solution)/shard_map/all_gather | solution.py:158
  21.6 14.1 %copy-start.9 = (s32[8]{0:T(128)}, s32[8]{0:T(128)S(1)}, u32[]{:S(2)}) copy-start(s32[8]{0:T(128)S(1)} %dynamic-slice_bitcast_fusion) | copy-start | bytes 100
  21.8 45.1 %copy-start.7 = (pred[256,256]{0,1:T(8,128)(4,1)}, pred[256,256]{0,1:T(8,128)(4,1)S(1)}, u32[]{:S(2)}) copy-start(pred[256,256]{0,1:T(8,128)(4,1)S(1)} %fusion.34) | copy-start | bytes 196612
  21.8 7.9 %copy-start.2 = (bf16[4096,256]{1,0:T(8,128)(2,1)S(1)}, bf16[4096,256]{1,0:T(8,128)(2,1)}, u32[]{:S(2)}) copy-start(bf16[4096,256]{1,0:T(8,128)(2,1)} %param.12) | copy-start | bytes 6291460
  29.7 2.4 %copy-start.3 = (bf16[4096,256]{1,0:T(8,128)(2,1)S(1)}, bf16[4096,256]{1,0:T(8,128)(2,1)}, u32[]{:S(2)}) copy-start(bf16[4096,256]{1,0:T(8,128)(2,1)} %param.13) | copy-start | bytes 6291460
  36.4 4.1 %copy-start.11 = (f32[4096]{0:T(1024)S(1)}, f32[4096]{0:T(1024)}, u32[]{:S(2)}) copy-start(f32[4096]{0:T(1024)} %param.10) | copy-start | bytes 49156
  37.4 83.9 %reduce-scatter.5.cloned.1.call-start = ((), (), s32[]{:S(2)}) async-start(), calls=%async_computation.7 | async-start | bytes 2621440 | tf_op jit(solution)/shard_map/reduce_scatter | solution.py:197
  38.2 2.3 %copy-start.4 = (bf16[256,4096]{1,0:T(8,128)(2,1)S(1)}, bf16[256,4096]{1,0:T(8,128)(2,1)}, u32[]{:S(2)}) copy-start(bf16[256,4096]{1,0:T(8,128)(2,1)} %all-gather.5.cloned.1.call-done) | copy-start | bytes 6291460
  47.4 1.2 copy-start.5
  48.6 0.9 slice-start
  66.8 2.4 %copy-start.13 = (f32[2,256,256,4]{2,1,3,0:T(8,128)S(1)}, f32[2,256,256,4]{2,1,3,0:T(8,128)}, u32[]{:S(2)}) copy-start(f32[2,256,256,4]{2,1,3,0:T(8,128)} %get-tuple-element.23) | copy-start | bytes 6291460
  69.2 1.6 copy-start.8
  75.0 0.9 copy-start.6
  89.7 65.6 %reduce-scatter.3.cloned.1.call-start = ((), (), s32[]{:S(2)}) async-start(), calls=%async_computation.5 | async-start | bytes 2621440 | tf_op jit(solution)/shard_map/reduce_scatter | solution.py:116
  96.9 24.4 %copy-start = (bf16[256,1024]{1,0:T(8,128)(2,1)S(1)}, bf16[256,1024]{1,0:T(8,128)(2,1)}, u32[]{:S(2)}) copy-start(bf16[256,1024]{1,0:T(8,128)(2,1)} %param.9) | copy-start | bytes 1572868
  96.9 58.4 %copy-start.1 = (bf16[256,1024]{1,0:T(8,128)(2,1)S(1)}, bf16[256,1024]{1,0:T(8,128)(2,1)}, u32[]{:S(2)}) copy-start(bf16[256,1024]{1,0:T(8,128)(2,1)} %reshape.235) | copy-start | bytes 1572868
  155.3 2.7 %copy-start.10 = (s32[8]{0:T(128)S(1)}, s32[8]{0:T(128)}, u32[]{:S(2)}) copy-start(s32[8]{0:T(128)} %copy-done.9) | copy-start | bytes 100
Sparse Core Ops, SparseCore 0:
  9.6 25.2 all-gather.4
  37.5 22.6 all-gather.6
  89.9 31.4 reduce-scatter.4
  123.9 31.3 reduce-scatter.2
